TPU v7x, 32 devices: a whole 2x2x4 slice. The times are simulated.
32 devices in a mesh: parts: 2 (over y), ctx: 8 (over z, x), tp: 2 (over core).
Axes of the slice: x: 2, y: 2, z: 4, core: 2. Of those that a mesh axis runs over, the one named last changes fastest.
Arguments:
- queries: bfloat16 [2048, 8192], P(('parts', 'ctx'), 'tp'), parts along dimension 0, may hold values from -9 to 9
- episode_key_cache: bfloat16 [128, 16, 1024], P(None, ('parts', 'ctx'), 'tp'), parts along dimension 1, may hold values from -9 to 9
- episode_value_cache: bfloat16 [128, 16, 1024], P(None, ('parts', 'ctx'), 'tp'), parts along dimension 1, may hold values from -6 to 6
- output_gradient: bfloat16 [2048, 8192], P(('parts', 'ctx'), 'tp'), parts along dimension 0, may hold values from -6 to 6
- block_lists: int32 [16, 2], P(('parts', 'ctx')), parts along dimension 0, may hold values from 0 to 7, as said below
- block_counts: int32 [16], P(('parts', 'ctx')), parts along dimension 0, may hold values from 1 to 2
Outputs:
- attn_out: bfloat16 [2048, 8192], P(('parts', 'ctx'), 'tp'), parts along dimension 0
- query_grad: bfloat16 [2048, 8192], P(('parts', 'ctx'), 'tp'), parts along dimension 0
- key_cache_gradient: bfloat16 [128, 16, 1024], P(None, ('parts', 'ctx'), 'tp'), parts along dimension 1
- value_cache_gradient: bfloat16 [128, 16, 1024], P(None, ('parts', 'ctx'), 'tp'), parts along dimension 1
There are 2 independent parts, one for each index of `parts`. A program takes and returns all parts, laid end to end along the dimension named above; each array names one. Nothing has to cross between parts.
Inputs may be any that keep to these rules, and one draw needn't show every extreme that they name: `block_lists`: each row names 2 different key blocks; a query block reads only its first block_counts entries.
All inputs are finite; a program needn't handle non-finite values.
Results may differ from a plain program's by a relative error of at most 0.0085.
The roundings to bfloat16 on the way count: a program that leaves them out, or rounds other values in their place, can miss the bound.
Values may be sent and summed in bfloat16 or wider, within the bound.
No kernel may reach another device: no remote copies, remote signals or barrier semaphores. Data moves between devices by JAX's collectives and lax.ppermute only.
A program may use at most 64 MiB of HBM per device.

v0:
```python
import jax
import jax.numpy as jnp
from jax import lax
from jax.sharding import PartitionSpec as P

QUERY_HEADS = 64
KEY_VALUE_HEADS = 8
HEAD_SIZE = 128
LIST = 2
TAG_COLUMNS = 128


def attend(query_part, key_part, value_part, grad_part, live_slots):
    score_scale = HEAD_SIZE ** (-0.5)
    scores = score_scale * jnp.einsum(
        "qgah,jkgh->gaqjk", query_part, key_part, preferred_element_type=jnp.float32
    )
    masked = jnp.where(live_slots[None, None, None, :, None], scores, -jnp.inf)
    row_peak = jnp.max(masked, axis=(3, 4), keepdims=True)
    exponent = jnp.exp(masked - row_peak)
    weights = exponent / jnp.sum(exponent, axis=(3, 4), keepdims=True)
    weights_low = weights.astype(jnp.bfloat16)
    attended = jnp.einsum(
        "gaqjk,jkgh->qgah", weights_low, value_part, preferred_element_type=jnp.float32
    ).astype(jnp.bfloat16)
    attended = lax.optimization_barrier(attended)
    row_delta = jnp.sum(grad_part.astype(jnp.float32) * attended.astype(jnp.float32), axis=3)
    weight_grad = jnp.einsum(
        "qgah,jkgh->gaqjk", grad_part, value_part, preferred_element_type=jnp.float32
    )
    score_grad = (
        weights * (weight_grad - jnp.transpose(row_delta, (1, 2, 0))[:, :, :, None, None])
    ).astype(jnp.bfloat16)
    query_grad = (
        score_scale
        * jnp.einsum("gaqjk,jkgh->qgah", score_grad, key_part, preferred_element_type=jnp.float32)
    ).astype(jnp.bfloat16)
    key_piece = score_scale * jnp.einsum(
        "gaqjk,qgah->jkgh", score_grad, query_part, preferred_element_type=jnp.float32
    )
    value_piece = jnp.einsum(
        "gaqjk,qgah->jkgh", weights_low, grad_part, preferred_element_type=jnp.float32
    )
    return (attended, query_grad, key_piece, value_piece)


def make_shards(peers):

    def shards(
        queries, episode_key_cache, episode_value_cache, output_gradient, block_lists, block_counts
    ):
        row_count = episode_key_cache.shape[0]
        key_width = episode_key_cache.shape[2]
        both_width = 2 * key_width
        chunk_rows = row_count // peers
        local_groups = key_width // HEAD_SIZE
        queries_per_group = QUERY_HEADS // KEY_VALUE_HEADS
        query_rows = queries.shape[0]
        held = jnp.concatenate([episode_key_cache[:, 0, :], episode_value_cache[:, 0, :]], axis=1)
        tag = jnp.concatenate([block_lists[0], block_counts]).astype(jnp.bfloat16)
        tag_block = jnp.zeros((row_count, TAG_COLUMNS), jnp.bfloat16)
        tag_block = tag_block.at[:, : LIST + 1].set(jnp.broadcast_to(tag, (row_count, LIST + 1)))
        first_send = jnp.concatenate([held, tag_block], axis=1).reshape(
            peers, chunk_rows, both_width + TAG_COLUMNS
        )
        first_recv = lax.all_to_all(first_send, "ctx", 0, 0, tiled=True)
        info = first_recv[:, 0, both_width : both_width + LIST + 1].astype(jnp.int32)
        lists_all = info[:, :LIST]
        counts_all = info[:, LIST]
        rows_held = first_recv[:, :, :both_width]
        picked = jnp.take(rows_held, lists_all, axis=0, mode="clip")
        fetched = lax.all_to_all(picked, "ctx", 0, 2, tiled=True)[0]
        key_rows = fetched[:, :, :key_width].reshape(LIST, row_count, local_groups, HEAD_SIZE)
        value_rows = fetched[:, :, key_width:].reshape(LIST, row_count, local_groups, HEAD_SIZE)
        live_slots = jnp.arange(LIST, dtype=jnp.int32) < block_counts[0]
        query_part = queries.reshape(query_rows, local_groups, queries_per_group, HEAD_SIZE)
        grad_part = output_gradient.reshape(query_rows, local_groups, queries_per_group, HEAD_SIZE)
        attended, query_grad, key_piece, value_piece = attend(
            query_part, key_rows, value_rows, grad_part, live_slots
        )
        pieces = jnp.concatenate(
            [
                key_piece.reshape(LIST, row_count, key_width),
                value_piece.reshape(LIST, row_count, key_width),
            ],
            axis=2,
        ).astype(jnp.bfloat16)
        back = lax.all_to_all(
            pieces.reshape(LIST, peers, chunk_rows, both_width), "ctx", 1, 1, tiled=True
        )
        slot_live = jnp.arange(LIST, dtype=jnp.int32)[None, :] < counts_all[:, None]
        selector = (
            (lists_all[:, :, None] == jnp.arange(peers, dtype=jnp.int32)[None, None, :])
            & slot_live[:, :, None]
        ).astype(jnp.bfloat16)
        summed = jnp.einsum(
            "jqrc,qjn->nrc", back, selector, preferred_element_type=jnp.float32
        ).astype(jnp.bfloat16)
        owned = lax.all_to_all(summed, "ctx", 0, 0, tiled=True).reshape(row_count, both_width)
        key_cache_gradient = owned[:, None, :key_width]
        value_cache_gradient = owned[:, None, key_width:]
        attn_out = attended.reshape(query_rows, local_groups * queries_per_group * HEAD_SIZE)
        query_grad = query_grad.reshape(query_rows, local_groups * queries_per_group * HEAD_SIZE)
        return (attn_out, query_grad, key_cache_gradient, value_cache_gradient)

    return shards


def solution(mesh):
    placed = (
        P(("parts", "ctx"), "tp"),
        P(None, ("parts", "ctx"), "tp"),
        P(None, ("parts", "ctx"), "tp"),
        P(("parts", "ctx"), "tp"),
        P(("parts", "ctx"), None),
        P(("parts", "ctx")),
    )
    return jax.shard_map(
        make_shards(mesh.shape["ctx"]),
        mesh=mesh,
        in_specs=placed,
        out_specs=(
            P(("parts", "ctx"), "tp"),
            P(("parts", "ctx"), "tp"),
            P(None, ("parts", "ctx"), "tp"),
            P(None, ("parts", "ctx"), "tp"),
        ),
        check_vma=False,
    )
```

profile of v0, /device:TPU:0, one launch (start us, length us, event | category | flops | bytes accessed | tf_op | source)
XLA Modules:
  0.0 88.5 jit_solution(7649527728791196662)
XLA Ops:
  0.6 0.0 copy-start.1
  0.6 0.6 compare_reduce_fusion
  1.9 0.7 convert_bitcast_fusion
  2.6 0.7 broadcast_select_fusion
  3.3 1.0 %maximum_maximum_fusion = bf16[8,16,1152]{2,1,0:T(8,128)(2,1)S(1)} fusion(bf16[8,16,512]{2,1,0:T(8,128)(2,1)} %bitcast.124, bf16[8,16,512]{2,1,0:T(8,128)(2,1)} %bitcast.125, bf16[1152]{0:T(1024)(128)(2,1)S(1)} %fusion.34), kind=kLoop, calls=%fused_computation.33 | loop fusion | flops 884736 | bytes 559360 | tf_op jit(solution)/shard_map/concatenate | solution.py:63
  4.4 17.4 %all_to_all.30 = bf16[8,16,1152]{2,1,0:T(8,128)(2,1)S(1)} all-to-all(bf16[8,16,1152]{2,1,0:T(8,128)(2,1)S(1)} %maximum_maximum_fusion), channel_id=1, replica_groups=mesh['parts'=2,'ctx'=8,'tp'=2] {'ctx'}, dimensions={0} | all-to-all | bytes 589824 | tf_op jit(solution)/shard_map/all_to_all | solution.py:66
  21.8 0.1 copy.175
  21.9 0.1 copy.119
  22.0 0.1 reshape.111
  22.1 1.4 %gather_fusion = bf16[16,16,1024]{2,1,0:T(8,128)(2,1)} fusion(bf16[8,16,1024]{2,1,0:T(8,128)(2,1)S(1)} %slice.53, s32[1024]{0:T(1024)S(1)} %pad_clamp_fusion), kind=kCustom, calls=%fused_computation | custom fusion | bytes 1048640 | tf_op jit(solution)/shard_map/jit(_take)/gather | solution.py:71
  23.5 3.5 %all-to-all-start.1 = ((bf16[8,2,16,1024]{3,2,1,0:T(8,128)(2,1)}), bf16[8,2,16,1024]{3,2,1,0:T(8,128)(2,1)S(1)}, u32[]{:S(2)}, u32[]{:S(2)}) async-start(bf16[8,2,16,1024]{3,2,1,0:T(8,128)(2,1)} %bitcast.3), calls=%async_computation.1 | async-start | bytes 1048576 | tf_op jit(solution)/shard_map/all_to_all | solution.py:72
  27.0 0.0 copy-done.1
  27.0 0.7 copy.127
  27.7 1.4 %copy.176 = bf16[16,8,32,128]{3,2,1,0:T(8,128)(2,1)S(1)} copy(bf16[16,8,32,128]{3,1,2,0:T(8,128)(2,1)} %bitcast.119) | data formatting | bytes 2097152
  29.1 11.6 %all-to-all-done.1 = bf16[8,2,16,1024]{3,2,1,0:T(8,128)(2,1)S(1)} async-done(((bf16[8,2,16,1024]{3,2,1,0:T(8,128)(2,1)}), bf16[8,2,16,1024]{3,2,1,0:T(8,128)(2,1)S(1)}, u32[]{:S(2)}, u32[]{:S(2)}) %all-to-all-start.1) | async-done | bytes 524320 | tf_op jit(solution)/shard_map/all_to_all | solution.py:72
  40.8 0.8 copy.121
  41.7 0.2 copy.122
  41.9 1.1 %bitcast_reduce_fusion = (f32[4,8,128]{2,1,0:T(8,128)S(1)}, f32[4,2,128,128,8]{3,2,4,1,0:T(8,128)S(1)}) fusion(pred[2]{0:T(512)(128)(4,1)S(1)} %iota_compare_fusion.3, bf16[128,4,8,128,1]{3,2,1,0,4:T(8,128)(2,1)S(1)} %bitcast.113, bf16[2,128,4,128,1]{1,3,2,0,4:T(8,128)(2,1)S(1)} %bitcast.117), kind=kOutput, calls=%fused_computation.5 | convolution fusion | flops 271577088 | bytes 5521410 | tf_op jit(solution)/shard_map/qgah,jkgh->gaqjk/dot_general | solution.py:15
  42.9 0.0 copy-start
  42.9 1.0 %fusion.4 = f32[4,8,128]{2,1,0:T(8,128)S(1)} fusion(f32[4,2,128,128,8]{3,2,4,1,0:T(8,128)S(1)} %get-tuple-element.45, f32[4,8,128]{2,1,0:T(8,128)S(1)} %get-tuple-element.44, pred[2]{0:T(512)(128)(4,1)S(1)} %iota_compare_fusion.3), kind=kLoop, calls=%fused_computation.9 | loop fusion | flops 4190208 | bytes 4227074 | tf_op jit(solution)/shard_map/reduce_sum | solution.py:21
  43.9 0.0 copy-start.3
  43.9 1.1 %fusion.37 = bf16[4,8,128,2,128]{2,4,1,3,0:T(8,128)(2,1)S(1)} fusion(f32[4,8,128]{2,1,0:T(8,128)S(1)} %fusion.4, f32[4,8,128]{2,1,0:T(8,128)S(1)} %get-tuple-element.44, f32[4,2,128,128,8]{3,2,4,1,0:T(8,128)S(1)} %get-tuple-element.45, pred[2]{0:T(512)(128)(4,1)S(1)} %iota_compare_fusion.3), kind=kLoop, calls=%fused_computation.55 | loop fusion | flops 5242880 | bytes 6324226 | tf_op jit(solution)/shard_map/convert_element_type | solution.py:22
  45.0 0.0 copy-done
  45.0 0.7 fusion.21
  45.7 0.0 copy-done.3
  45.7 0.5 fusion.14
  46.2 0.9 %copy.135 = bf16[2,128,4,128]{3,2,1,0:T(4,128)(2,1)} copy(bf16[2,128,4,128]{3,1,0,2:T(8,128)(2,1)S(1)} %fusion.21) | data formatting | bytes 524288 | tf_op jit(solution)/shard_map/gaqjk,qgah->jkgh/transpose | solution.py:41
  47.1 1.7 %concatenate.31 = bf16[2,8,16,512]{3,2,1,0:T(8,128)(2,1)} reshape(bf16[2,128,4,128]{3,2,1,0:T(4,128)(2,1)} %copy.135) | data formatting | bytes 524288 | tf_op jit(solution)/shard_map/concatenate | solution.py:81
  48.8 0.4 multiply_reduce_fusion
  49.2 3.9 %fusion.1 = bf16[4,8,128,2,128]{2,4,1,3,0:T(8,128)(2,1)S(1)} fusion(bf16[128,4,8,128,1]{0,3,2,4,1:T(8,128)(2,1)S(1)} %bitcast.112, f32[4,8,128]{2,1,0:T(8,128)S(1)} %bitcast.126, bf16[2,128,4,128,1]{1,3,2,0,4:T(8,128)(2,1)} %bitcast.122, f32[4,8,128]{2,1,0:T(8,128)S(1)} %fusion.4, f32[4,8,128]{2,1,0:T(8,128)S(1)} %get-tuple-element.44, ...), kind=kOutput, calls=%fused_computation.3 | convolution fusion | flops 275775488 | bytes 7651330 | tf_op jit(solution)/shard_map/qgah,jkgh->gaqjk/dot_general | solution.py:28
  53.1 0.0 copy-start.4
  53.2 0.8 fusion.22
  54.0 0.5 copy-done.4
  54.5 0.2 copy.133
  54.7 0.1 concatenate.30
  54.8 0.0 copy-done.2
  54.8 0.1 pad_maximum_fusion
  54.9 1.3 %copy.136 = bf16[2,8,16,1024]{3,0,2,1:T(2,128)(2,1)} copy(bf16[2,8,16,1024]{3,2,1,0:T(8,128)(2,1)S(1)} %pad_maximum_fusion) | data formatting | bytes 1048576 | tf_op jit(solution)/shard_map/concatenate | solution.py:81
  56.2 3.6 %all-to-all-start.2 = ((bf16[2,8,16,1024]{3,0,2,1:T(2,128)(2,1)}), bf16[2,8,16,1024]{3,0,2,1:T(2,128)(2,1)S(1)}, u32[]{:S(2)}, u32[]{:S(2)}) async-start(bf16[2,8,16,1024]{3,0,2,1:T(2,128)(2,1)} %copy.136), calls=%async_computation.2 | async-start | bytes 1048576 | tf_op jit(solution)/shard_map/all_to_all | solution.py:88
  59.9 14.2 %all-to-all-done.2 = bf16[2,8,16,1024]{3,0,2,1:T(2,128)(2,1)S(1)} async-done(((bf16[2,8,16,1024]{3,0,2,1:T(2,128)(2,1)}), bf16[2,8,16,1024]{3,0,2,1:T(2,128)(2,1)S(1)}, u32[]{:S(2)}, u32[]{:S(2)}) %all-to-all-start.2) | async-done | bytes 524320 | tf_op jit(solution)/shard_map/all_to_all | solution.py:88
  74.0 0.4 fusion.20
  74.4 0.9 copy.138
  75.3 3.6 %all-to-all-start.3 = ((bf16[8,16,1024]{2,1,0:T(8,128)(2,1)}), bf16[8,16,1024]{2,1,0:T(8,128)(2,1)S(1)}, u32[]{:S(2)}, u32[]{:S(2)}) async-start(bf16[8,16,1024]{2,1,0:T(8,128)(2,1)} %copy.138), calls=%async_computation.3 | async-start | bytes 524288 | tf_op jit(solution)/shard_map/all_to_all | solution.py:99
  78.9 2.1 %fusion.5 = bf16[4,128,8,128]{3,1,2,0:T(8,128)(2,1)S(1)} fusion(bf16[4,8,128,2,128]{2,4,1,3,0:T(8,128)(2,1)} %copy-done.4, bf16[2,128,4,128,1]{1,3,2,0,4:T(8,128)(2,1)S(1)} %bitcast.118), kind=kOutput, calls=%fused_computation.11 | convolution fusion | flops 269484032 | bytes 3407872 | tf_op jit(solution)/shard_map/gaqjk,jkgh->qgah/dot_general | solution.py:36
  81.0 1.3 %copy.140 = bf16[128,4096]{1,0:T(8,128)(2,1)} copy(bf16[128,4096]{0,1:T(8,128)(2,1)S(1)} %bitcast.120) | data formatting | bytes 2097152
  82.4 1.3 %copy.139 = bf16[128,4096]{1,0:T(8,128)(2,1)} copy(bf16[128,4096]{0,1:T(8,128)(2,1)S(1)} %bitcast.110) | data formatting | bytes 2097152
  83.7 4.1 %all-to-all-done.3 = bf16[8,16,1024]{2,1,0:T(8,128)(2,1)S(1)} async-done(((bf16[8,16,1024]{2,1,0:T(8,128)(2,1)}), bf16[8,16,1024]{2,1,0:T(8,128)(2,1)S(1)}, u32[]{:S(2)}, u32[]{:S(2)}) %all-to-all-start.3) | async-done | bytes 262176 | tf_op jit(solution)/shard_map/all_to_all | solution.py:99
  87.8 0.7 slice_bitcast_fusion
  (13 shorter events, 0.2 us)
Async XLA Ops:
  0.6 26.4 %copy-start.1 = (bf16[128,4096]{1,0:T(8,128)(2,1)S(1)}, bf16[128,4096]{1,0:T(8,128)(2,1)}, u32[]{:S(2)}) copy-start(bf16[128,4096]{1,0:T(8,128)(2,1)} %param.11) | copy-start | bytes 3145732
  23.5 17.3 %all-to-all-start.1 = ((bf16[8,2,16,1024]{3,2,1,0:T(8,128)(2,1)}), bf16[8,2,16,1024]{3,2,1,0:T(8,128)(2,1)S(1)}, u32[]{:S(2)}, u32[]{:S(2)}) async-start(bf16[8,2,16,1024]{3,2,1,0:T(8,128)(2,1)} %bitcast.3), calls=%async_computation.1 | async-start | bytes 1048576 | tf_op jit(solution)/shard_map/all_to_all | solution.py:72
  42.9 2.1 %copy-start = (f32[4,2,128,128,8]{3,2,4,1,0:T(8,128)}, f32[4,2,128,128,8]{3,2,4,1,0:T(8,128)S(1)}, u32[]{:S(2)}) copy-start(f32[4,2,128,128,8]{3,2,4,1,0:T(8,128)S(1)} %get-tuple-element.45) | copy-start | bytes 12582916
  43.9 1.8 %copy-start.3 = (bf16[2,128,512]{1,2,0:T(8,128)(2,1)S(1)}, bf16[2,128,512]{1,2,0:T(8,128)(2,1)}, u32[]{:S(2)}) copy-start(bf16[2,128,512]{1,2,0:T(8,128)(2,1)} %copy.121) | copy-start | bytes 786436
  53.1 1.3 %copy-start.4 = (bf16[4,8,128,2,128]{2,4,1,3,0:T(8,128)(2,1)}, bf16[4,8,128,2,128]{2,4,1,3,0:T(8,128)(2,1)S(1)}, u32[]{:S(2)}) copy-start(bf16[4,8,128,2,128]{2,4,1,3,0:T(8,128)(2,1)S(1)} %fusion.1) | copy-start | bytes 6291460
  53.1 1.6 %copy-start.2 = (bf16[2,8,16,512]{3,2,1,0:T(8,128)(2,1)S(1)}, bf16[2,8,16,512]{3,2,1,0:T(8,128)(2,1)}, u32[]{:S(2)}) copy-start(bf16[2,8,16,512]{3,2,1,0:T(8,128)(2,1)} %concatenate.31) | copy-start | bytes 786436
  56.2 17.8 %all-to-all-start.2 = ((bf16[2,8,16,1024]{3,0,2,1:T(2,128)(2,1)}), bf16[2,8,16,1024]{3,0,2,1:T(2,128)(2,1)S(1)}, u32[]{:S(2)}, u32[]{:S(2)}) async-start(bf16[2,8,16,1024]{3,0,2,1:T(2,128)(2,1)} %copy.136), calls=%async_computation.2 | async-start | bytes 1048576 | tf_op jit(solution)/shard_map/all_to_all | solution.py:88
  75.3 12.5 %all-to-all-start.3 = ((bf16[8,16,1024]{2,1,0:T(8,128)(2,1)}), bf16[8,16,1024]{2,1,0:T(8,128)(2,1)S(1)}, u32[]{:S(2)}, u32[]{:S(2)}) async-start(bf16[8,16,1024]{2,1,0:T(8,128)(2,1)} %copy.138), calls=%async_computation.3 | async-start | bytes 524288 | tf_op jit(solution)/shard_map/all_to_all | solution.py:99
where the time goes:
time: 89.1 us; the launch traced here: 88.5 us
  waiting for transfers between devices  29.9 us (34%)
  blocking collectives  17.4 us (20%)
  local copies, waits for them, and re-layouts  13.9 us (16%)
  starting transfers between devices  10.8 us (12%)
  matrix products  9.43 us (11%)
  other arithmetic  5.54 us (6%)
  between operations  1.53 us (2%)
    all_to_all x1, blocking collectives, shards(): first_recv = lax.all_to_all(first_send, 'ctx', 0, 0, tiled=True)  17.4 us
    all_to_all x1, waiting for transfers between devices, shards(): lax.all_to_all(pieces.reshape(LIST, peers, chunk_rows, both_width), 'ctx'...  14.2 us
    all_to_all x1, waiting for transfers between devices, shards(): fetched = lax.all_to_all(picked, 'ctx', 0, 2, tiled=True)[0]  11.6 us
    unnamed x16, local copies, waits for them, and re-layouts  5.36 us
    all_to_all x1, waiting for transfers between devices, shards(): lax.all_to_all(summed, 'ctx', 0, 0, tiled=True)  4.13 us
    dot_general x1, matrix products, attend(): jnp.einsum('qgah,jkgh->gaqjk', grad_part, value_part, preferred_element_t...  3.92 us
    all_to_all x1, starting transfers between devices, shards(): lax.all_to_all(pieces.reshape(LIST, peers, chunk_rows, both_width), 'ctx'...  3.64 us
    all_to_all x1, starting transfers between devices, shards(): lax.all_to_all(summed, 'ctx', 0, 0, tiled=True)  3.63 us
  transfers between devices with their start and end apart: 3, of which 3 were waited for; matrix products, arithmetic and copies ran while one was open for 8% of the time, Pallas kernels for 0%

commit v1 on v0

--- a/solution.py
+++ b/solution.py
@@ -85,8 +85,20 @@
             ],
             axis=2,
         ).astype(jnp.bfloat16)
-        back = lax.all_to_all(
-            pieces.reshape(LIST, peers, chunk_rows, both_width), "ctx", 1, 1, tiled=True
+        back = jnp.concatenate(
+            lax.all_to_all(
+                jnp.stack(
+                    jnp.split(
+                        pieces.reshape(LIST, peers, chunk_rows, both_width),
+                        lax.axis_size("ctx"),
+                        axis=1,
+                    )
+                ),
+                "ctx",
+                0,
+                0,
+            ),
+            axis=1,
         )
         slot_live = jnp.arange(LIST, dtype=jnp.int32)[None, :] < counts_all[:, None]
         selector = (

time: 89.1 us -> 89.2 us (level)
    another operation x0 -> x2, local copies, waits for them, and re-layouts: none -> 1.34 us  [shards(): jnp.stack(jnp.split(pieces.reshape(LIST, peers, chunk_rows, both_width),...]
    concatenate x3, local copies, waits for them, and re-layouts: 3.18 us -> 1.87 us  [shards(): jnp.concatenate([key_piece.reshape(LIST, row_count, key_width), value_pie...]
    unnamed x16 -> x24, local copies, waits for them, and re-layouts: 5.36 us -> 5.43 us
where the time goes in v1:
time: 89.2 us; the launch traced here: 88.6 us
  waiting for transfers between devices  29.9 us (34%)
  blocking collectives  17.4 us (20%)
  local copies, waits for them, and re-layouts  14 us (16%)
  starting transfers between devices  10.8 us (12%)
  matrix products  9.45 us (11%)
  other arithmetic  5.48 us (6%)
  between operations  1.6 us (2%)
    all_to_all x1, blocking collectives, shards(): first_recv = lax.all_to_all(first_send, 'ctx', 0, 0, tiled=True)  17.4 us
    all_to_all x1, waiting for transfers between devices, shards(): lax.all_to_all(jnp.stack(jnp.split(pieces.reshape(LIST, peers, chunk_rows...  14.2 us
    all_to_all x1, waiting for transfers between devices, shards(): fetched = lax.all_to_all(picked, 'ctx', 0, 2, tiled=True)[0]  11.6 us
    unnamed x24, local copies, waits for them, and re-layouts  5.43 us
    all_to_all x1, waiting for transfers between devices, shards(): lax.all_to_all(summed, 'ctx', 0, 0, tiled=True)  4.13 us
    dot_general x1, matrix products, attend(): jnp.einsum('qgah,jkgh->gaqjk', grad_part, value_part, preferred_element_t...  3.92 us
    all_to_all x1, starting transfers between devices, shards(): lax.all_to_all(jnp.stack(jnp.split(pieces.reshape(LIST, peers, chunk_rows...  3.63 us
    all_to_all x1, starting transfers between devices, shards(): lax.all_to_all(summed, 'ctx', 0, 0, tiled=True)  3.63 us
  transfers between devices with their start and end apart: 3, of which 3 were waited for; matrix products, arithmetic and copies ran while one was open for 8% of the time, Pallas kernels for 0%

profile of v1, /device:TPU:0, one launch (start us, length us, event | category | flops | bytes accessed | tf_op | source)
XLA Modules:
  0.0 88.6 jit_solution(13531339385126337616)
XLA Ops:
  0.6 0.0 copy-start.1
  0.6 0.6 compare_reduce_fusion
  1.9 0.7 convert_bitcast_fusion
  2.6 0.7 broadcast_select_fusion
  3.3 1.0 %maximum_maximum_fusion = bf16[8,16,1152]{2,1,0:T(8,128)(2,1)S(1)} fusion(bf16[8,16,512]{2,1,0:T(8,128)(2,1)} %bitcast.161, bf16[8,16,512]{2,1,0:T(8,128)(2,1)} %bitcast.162, bf16[1152]{0:T(1024)(128)(2,1)S(1)} %fusion.43), kind=kLoop, calls=%fused_computation.33 | loop fusion | flops 884736 | bytes 559360 | tf_op jit(solution)/shard_map/concatenate | solution.py:63
  4.4 17.4 %all_to_all.30 = bf16[8,16,1152]{2,1,0:T(8,128)(2,1)S(1)} all-to-all(bf16[8,16,1152]{2,1,0:T(8,128)(2,1)S(1)} %maximum_maximum_fusion), channel_id=1, replica_groups=mesh['parts'=2,'ctx'=8,'tp'=2] {'ctx'}, dimensions={0} | all-to-all | bytes 589824 | tf_op jit(solution)/shard_map/all_to_all | solution.py:66
  21.8 0.1 copy.426
  21.9 0.1 copy.370
  22.0 0.1 reshape.119
  22.1 1.4 %gather_fusion = bf16[16,16,1024]{2,1,0:T(8,128)(2,1)} fusion(bf16[8,16,1024]{2,1,0:T(8,128)(2,1)S(1)} %slice.53, s32[1024]{0:T(1024)S(1)} %pad_clamp_fusion), kind=kCustom, calls=%fused_computation | custom fusion | bytes 1048640 | tf_op jit(solution)/shard_map/jit(_take)/gather | solution.py:71
  23.5 3.5 %all-to-all-start.1 = ((bf16[8,2,16,1024]{3,2,1,0:T(8,128)(2,1)}), bf16[8,2,16,1024]{3,2,1,0:T(8,128)(2,1)S(1)}, u32[]{:S(2)}, u32[]{:S(2)}) async-start(bf16[8,2,16,1024]{3,2,1,0:T(8,128)(2,1)} %bitcast.3), calls=%async_computation.1 | async-start | bytes 1048576 | tf_op jit(solution)/shard_map/all_to_all | solution.py:72
  27.0 0.0 copy-done.1
  27.0 0.7 copy.378
  27.7 1.4 %copy.427 = bf16[16,8,32,128]{3,2,1,0:T(8,128)(2,1)S(1)} copy(bf16[16,8,32,128]{3,1,2,0:T(8,128)(2,1)} %bitcast.156) | data formatting | bytes 2097152
  29.1 11.6 %all-to-all-done.1 = bf16[8,2,16,1024]{3,2,1,0:T(8,128)(2,1)S(1)} async-done(((bf16[8,2,16,1024]{3,2,1,0:T(8,128)(2,1)}), bf16[8,2,16,1024]{3,2,1,0:T(8,128)(2,1)S(1)}, u32[]{:S(2)}, u32[]{:S(2)}) %all-to-all-start.1) | async-done | bytes 524320 | tf_op jit(solution)/shard_map/all_to_all | solution.py:72
  40.8 0.8 copy.372
  41.7 0.2 copy.373
  41.9 1.1 %bitcast_reduce_fusion = (f32[4,8,128]{2,1,0:T(8,128)S(1)}, f32[4,2,128,128,8]{3,2,4,1,0:T(8,128)S(1)}) fusion(pred[2]{0:T(512)(128)(4,1)S(1)} %iota_compare_fusion.3, bf16[128,4,8,128,1]{3,2,1,0,4:T(8,128)(2,1)S(1)} %bitcast.150, bf16[2,128,4,128,1]{1,3,2,0,4:T(8,128)(2,1)S(1)} %bitcast.154), kind=kOutput, calls=%fused_computation.5 | convolution fusion | flops 271577088 | bytes 5521410 | tf_op jit(solution)/shard_map/qgah,jkgh->gaqjk/dot_general | solution.py:15
  42.9 0.0 copy-start
  42.9 1.0 %fusion.4 = f32[4,8,128]{2,1,0:T(8,128)S(1)} fusion(f32[4,2,128,128,8]{3,2,4,1,0:T(8,128)S(1)} %get-tuple-element.73, f32[4,8,128]{2,1,0:T(8,128)S(1)} %get-tuple-element.72, pred[2]{0:T(512)(128)(4,1)S(1)} %iota_compare_fusion.3), kind=kLoop, calls=%fused_computation.9 | loop fusion | flops 4190208 | bytes 4227074 | tf_op jit(solution)/shard_map/reduce_sum | solution.py:21
  43.9 0.0 copy-start.3
  43.9 1.1 %fusion.46 = bf16[4,8,128,2,128]{2,4,1,3,0:T(8,128)(2,1)S(1)} fusion(f32[4,8,128]{2,1,0:T(8,128)S(1)} %fusion.4, f32[4,8,128]{2,1,0:T(8,128)S(1)} %get-tuple-element.72, f32[4,2,128,128,8]{3,2,4,1,0:T(8,128)S(1)} %get-tuple-element.73, pred[2]{0:T(512)(128)(4,1)S(1)} %iota_compare_fusion.3), kind=kLoop, calls=%fused_computation.73 | loop fusion | flops 5242880 | bytes 6324226 | tf_op jit(solution)/shard_map/convert_element_type | solution.py:22
  45.0 0.0 copy-done
  45.0 0.7 fusion.21
  45.7 0.0 copy-done.3
  45.7 0.5 fusion.14
  46.2 0.9 %copy.386 = bf16[2,128,4,128]{3,2,1,0:T(4,128)(2,1)} copy(bf16[2,128,4,128]{3,1,0,2:T(8,128)(2,1)S(1)} %fusion.21) | data formatting | bytes 524288 | tf_op jit(solution)/shard_map/gaqjk,qgah->jkgh/transpose | solution.py:41
  47.1 1.7 %concatenate.31 = bf16[2,8,16,512]{3,2,1,0:T(8,128)(2,1)} reshape(bf16[2,128,4,128]{3,2,1,0:T(4,128)(2,1)} %copy.386) | data formatting | bytes 524288 | tf_op jit(solution)/shard_map/concatenate | solution.py:81
  48.8 0.4 multiply_reduce_fusion
  49.2 3.9 %fusion.1 = bf16[4,8,128,2,128]{2,4,1,3,0:T(8,128)(2,1)S(1)} fusion(bf16[128,4,8,128,1]{0,3,2,4,1:T(8,128)(2,1)S(1)} %bitcast.149, f32[4,8,128]{2,1,0:T(8,128)S(1)} %bitcast.163, bf16[2,128,4,128,1]{1,3,2,0,4:T(8,128)(2,1)} %bitcast.159, f32[4,8,128]{2,1,0:T(8,128)S(1)} %fusion.4, f32[4,8,128]{2,1,0:T(8,128)S(1)} %get-tuple-element.72, ...), kind=kOutput, calls=%fused_computation.3 | convolution fusion | flops 275775488 | bytes 7651330 | tf_op jit(solution)/shard_map/qgah,jkgh->gaqjk/dot_general | solution.py:28
  53.1 0.0 copy-start.4
  53.2 0.0 copy-start.2
  53.2 0.8 fusion.22
  54.0 0.5 copy-done.4
  54.5 0.2 copy.384
  54.7 0.1 concatenate.30
  54.8 0.0 copy-done.2
  55.0 1.3 %copy.387 = bf16[8,2,1,16,1024]{4,1,3,2,0:T(2,128)(2,1)} copy(bf16[8,2,1,16,1024]{4,3,1,2,0:T(8,128)(2,1)S(1)} %fusion.32) | data formatting | bytes 1048576 | tf_op jit(solution)/shard_map/stack | solution.py:90
  56.3 3.6 %all-to-all-start.2 = ((bf16[8,2,1,16,1024]{4,1,3,2,0:T(2,128)(2,1)}), bf16[8,2,1,16,1024]{4,1,3,2,0:T(2,128)(2,1)S(1)}, u32[]{:S(2)}, u32[]{:S(2)}) async-start(bf16[8,2,1,16,1024]{4,1,3,2,0:T(2,128)(2,1)} %copy.387), calls=%async_computation.2 | async-start | bytes 1048576 | tf_op jit(solution)/shard_map/all_to_all | solution.py:89
  60.0 14.2 %all-to-all-done.2 = bf16[8,2,1,16,1024]{4,1,3,2,0:T(2,128)(2,1)S(1)} async-done(((bf16[8,2,1,16,1024]{4,1,3,2,0:T(2,128)(2,1)}), bf16[8,2,1,16,1024]{4,1,3,2,0:T(2,128)(2,1)S(1)}, u32[]{:S(2)}, u32[]{:S(2)}) %all-to-all-start.2) | async-done | bytes 524320 | tf_op jit(solution)/shard_map/all_to_all | solution.py:89
  74.1 0.4 fusion.20
  74.5 0.9 copy.389
  75.4 3.6 %all-to-all-start.3 = ((bf16[8,16,1024]{2,1,0:T(8,128)(2,1)}), bf16[8,16,1024]{2,1,0:T(8,128)(2,1)S(1)}, u32[]{:S(2)}, u32[]{:S(2)}) async-start(bf16[8,16,1024]{2,1,0:T(8,128)(2,1)} %copy.389), calls=%async_computation.3 | async-start | bytes 524288 | tf_op jit(solution)/shard_map/all_to_all | solution.py:111
  79.0 2.1 %fusion.5 = bf16[4,128,8,128]{3,1,2,0:T(8,128)(2,1)S(1)} fusion(bf16[4,8,128,2,128]{2,4,1,3,0:T(8,128)(2,1)} %copy-done.4, bf16[2,128,4,128,1]{1,3,2,0,4:T(8,128)(2,1)S(1)} %bitcast.155), kind=kOutput, calls=%fused_computation.11 | convolution fusion | flops 269484032 | bytes 3407872 | tf_op jit(solution)/shard_map/gaqjk,jkgh->qgah/dot_general | solution.py:36
  81.2 1.3 %copy.391 = bf16[128,4096]{1,0:T(8,128)(2,1)} copy(bf16[128,4096]{0,1:T(8,128)(2,1)S(1)} %bitcast.157) | data formatting | bytes 2097152
  82.5 1.3 %copy.390 = bf16[128,4096]{1,0:T(8,128)(2,1)} copy(bf16[128,4096]{0,1:T(8,128)(2,1)S(1)} %bitcast.147) | data formatting | bytes 2097152
  83.8 4.1 %all-to-all-done.3 = bf16[8,16,1024]{2,1,0:T(8,128)(2,1)S(1)} async-done(((bf16[8,16,1024]{2,1,0:T(8,128)(2,1)}), bf16[8,16,1024]{2,1,0:T(8,128)(2,1)S(1)}, u32[]{:S(2)}, u32[]{:S(2)}) %all-to-all-start.3) | async-done | bytes 262176 | tf_op jit(solution)/shard_map/all_to_all | solution.py:111
  87.9 0.7 slice_bitcast_fusion
  (22 shorter events, 0.3 us)
Async XLA Ops:
  0.6 26.4 %copy-start.1 = (bf16[128,4096]{1,0:T(8,128)(2,1)S(1)}, bf16[128,4096]{1,0:T(8,128)(2,1)}, u32[]{:S(2)}) copy-start(bf16[128,4096]{1,0:T(8,128)(2,1)} %param.11) | copy-start | bytes 3145732
  23.5 17.3 %all-to-all-start.1 = ((bf16[8,2,16,1024]{3,2,1,0:T(8,128)(2,1)}), bf16[8,2,16,1024]{3,2,1,0:T(8,128)(2,1)S(1)}, u32[]{:S(2)}, u32[]{:S(2)}) async-start(bf16[8,2,16,1024]{3,2,1,0:T(8,128)(2,1)} %bitcast.3), calls=%async_computation.1 | async-start | bytes 1048576 | tf_op jit(solution)/shard_map/all_to_all | solution.py:72
  42.9 2.1 %copy-start = (f32[4,2,128,128,8]{3,2,4,1,0:T(8,128)}, f32[4,2,128,128,8]{3,2,4,1,0:T(8,128)S(1)}, u32[]{:S(2)}) copy-start(f32[4,2,128,128,8]{3,2,4,1,0:T(8,128)S(1)} %get-tuple-element.73) | copy-start | bytes 12582916
  43.9 1.8 %copy-start.3 = (bf16[2,128,512]{1,2,0:T(8,128)(2,1)S(1)}, bf16[2,128,512]{1,2,0:T(8,128)(2,1)}, u32[]{:S(2)}) copy-start(bf16[2,128,512]{1,2,0:T(8,128)(2,1)} %copy.372) | copy-start | bytes 786436
  53.1 1.3 %copy-start.4 = (bf16[4,8,128,2,128]{2,4,1,3,0:T(8,128)(2,1)}, bf16[4,8,128,2,128]{2,4,1,3,0:T(8,128)(2,1)S(1)}, u32[]{:S(2)}) copy-start(bf16[4,8,128,2,128]{2,4,1,3,0:T(8,128)(2,1)S(1)} %fusion.1) | copy-start | bytes 6291460
  53.2 1.7 %copy-start.2 = (bf16[2,8,16,512]{3,2,1,0:T(8,128)(2,1)S(1)}, bf16[2,8,16,512]{3,2,1,0:T(8,128)(2,1)}, u32[]{:S(2)}) copy-start(bf16[2,8,16,512]{3,2,1,0:T(8,128)(2,1)} %concatenate.31) | copy-start | bytes 786436
  56.3 17.8 %all-to-all-start.2 = ((bf16[8,2,1,16,1024]{4,1,3,2,0:T(2,128)(2,1)}), bf16[8,2,1,16,1024]{4,1,3,2,0:T(2,128)(2,1)S(1)}, u32[]{:S(2)}, u32[]{:S(2)}) async-start(bf16[8,2,1,16,1024]{4,1,3,2,0:T(2,128)(2,1)} %copy.387), calls=%async_computation.2 | async-start | bytes 1048576 | tf_op jit(solution)/shard_map/all_to_all | solution.py:89
  75.4 12.5 %all-to-all-start.3 = ((bf16[8,16,1024]{2,1,0:T(8,128)(2,1)}), bf16[8,16,1024]{2,1,0:T(8,128)(2,1)S(1)}, u32[]{:S(2)}, u32[]{:S(2)}) async-start(bf16[8,16,1024]{2,1,0:T(8,128)(2,1)} %copy.389), calls=%async_computation.3 | async-start | bytes 524288 | tf_op jit(solution)/shard_map/all_to_all | solution.py:111
